TPU v7x, 512 devices: a whole 4x8x8 slice. The times are simulated.
512 devices in a mesh: ctx: 64 (over y, x, core), head: 8 (over z).
Axes of the slice: x: 4, y: 8, z: 8, core: 2. Of those that a mesh axis runs over, the one named last changes fastest.
Arguments:
- tokens: bfloat16 [65536, 2048], P('ctx', 'head'), may hold values from -6 to 6
- w_qkv: bfloat16 [3, 2048, 2048], P(None, 'ctx', 'head'), may hold values from -0.125 to 0.125
- out_gain: float32 [2048], P('head'), may hold values from 0.25 to 1.75
- seg_ids: int32 [65536], P('ctx'), may hold values from 0 to 15, never falling along the last dimension, each value on 1 to 16384 neighbouring positions
Outputs:
- attended: bfloat16 [65536, 2048], P('ctx', 'head')
Inputs may be any that keep to these rules, and one draw needn't show every extreme that they name: `seg_ids`: segment numbers never fall along the stream; each segment covers 1 to 16384 consecutive tokens, and one covers exactly 16384.
All inputs are finite; a program needn't handle non-finite values.
Results may differ from a plain program's by a relative error of at most 0.012.
Values may be sent and summed in bfloat16 or wider, within the bound.
No kernel may reach another device: no remote copies, remote signals or barrier semaphores. Data moves between devices by JAX's collectives and lax.ppermute only.
A program may use at most 64 MiB of HBM per device.

v0:
```python
import jax
import jax.numpy as jnp
from jax import lax
from jax.sharding import PartitionSpec as P

HEAD_DIM = 128


def passed_along(value, axis, steps):
    count = lax.axis_size(axis)
    leading, last = (max(0, -steps), min(count, count - steps))
    return lax.ppermute(value, axis, [(source, source + steps) for source in range(leading, last)])


def feature_map(values):
    return (jax.nn.elu(values.astype(jnp.float32)) + 1.0).astype(jnp.bfloat16)


def combine(earlier, later):
    first_state, first_tail = earlier
    later_state, later_tail = later
    linked = (first_tail == later_tail) | (later_tail < 0.0)
    return (
        later_state + jnp.where(linked, first_state, 0.0),
        jnp.where(later_tail < 0.0, first_tail, later_tail),
    )


def prepare(projected, segment):
    row_count = segment.shape[0]
    head_count = projected.shape[2] // HEAD_DIM
    queries = feature_map(projected[0]).reshape(row_count, head_count, HEAD_DIM)
    key_map = feature_map(projected[1]).reshape(row_count, head_count, HEAD_DIM)
    values = projected[2].reshape(row_count, head_count, HEAD_DIM)
    seg_float = segment.astype(jnp.float32)
    tail_id = seg_float[-1]
    key_tail = jnp.where((seg_float == tail_id)[:, None, None], key_map, jnp.zeros_like(key_map))
    kv_state = jnp.einsum("thd,the->hde", key_tail, values, preferred_element_type=jnp.float32)
    return (queries, key_map, values, seg_float, kv_state, tail_id)


def complete(queries, key_map, values, seg_float, state_in, tail_in, out_gain):
    row_count, head_count = (queries.shape[0], queries.shape[1])
    state_low = state_in.astype(jnp.bfloat16)
    prefix = jnp.einsum("thd,hde->the", queries, state_low, preferred_element_type=jnp.float32)
    prefix = jnp.where((seg_float == tail_in)[:, None, None], prefix, 0.0)
    block_rows = min(512, row_count)
    positions = jnp.arange(row_count, dtype=jnp.int32)

    def one_block(blk_no):
        first_row = blk_no * block_rows
        query_blk = lax.dynamic_slice_in_dim(queries, first_row, block_rows, 0)
        query_pos = first_row + jnp.arange(block_rows, dtype=jnp.int32)
        query_seg = lax.dynamic_slice_in_dim(seg_float, first_row, block_rows, 0)
        scores = jnp.einsum("bhd,shd->hbs", query_blk, key_map, preferred_element_type=jnp.float32)
        visible = (positions[None, :] <= query_pos[:, None]) & (
            seg_float[None, :] == query_seg[:, None]
        )
        weights = jnp.where(visible[None], scores, 0.0).astype(jnp.bfloat16)
        return jnp.einsum("hbs,she->bhe", weights, values, preferred_element_type=jnp.float32)

    local_part = lax.map(one_block, jnp.arange(row_count // block_rows, dtype=jnp.int32))
    numerator = local_part.reshape(row_count, head_count, HEAD_DIM) + prefix
    inv_norm = lax.rsqrt(jnp.mean(numerator * numerator, axis=-1, keepdims=True) + 1e-05)
    result = numerator * inv_norm * out_gain.reshape(head_count, HEAD_DIM)
    return result.astype(jnp.bfloat16).reshape(row_count, head_count * HEAD_DIM)


def per_device(tokens, w_qkv, out_gain, seg_ids):
    whole = lax.all_gather(tokens, "head", axis=1, tiled=True)
    projected = jnp.einsum(
        "tr,grc->gtc",
        whole,
        lax.all_gather(w_qkv, "ctx", axis=1, tiled=True),
        preferred_element_type=jnp.float32,
    ).astype(jnp.bfloat16)
    queries, key_map, values, seg_float, kv_state, tail_id = prepare(projected, seg_ids)
    empty_state = jnp.zeros_like(kv_state)
    own_pair = (kv_state, tail_id)

    def hand_round(turn_no, carried):
        running, _ = carried
        incoming = (
            passed_along(running[0].astype(jnp.bfloat16), "ctx", 1).astype(jnp.float32),
            passed_along(running[1].astype(jnp.bfloat16), "ctx", 1).astype(jnp.float32),
        )
        return (combine(incoming, own_pair), incoming)

    start_pair = (empty_state, jnp.array(-1.0, jnp.float32))
    _, arrived = lax.fori_loop(0, lax.axis_size("ctx") - 1, hand_round, (own_pair, start_pair))
    state_in, tail_in = arrived
    return complete(queries, key_map, values, seg_float, state_in, tail_in, out_gain)


def solution(mesh):
    placed = (P("ctx", "head"), P(None, "ctx", "head"), P("head"), P("ctx"))
    return jax.shard_map(
        per_device, mesh=mesh, in_specs=placed, out_specs=P("ctx", "head"), check_vma=False
    )
```

profile of v0, /device:TPU:32, one launch (start us, length us, event | category | flops | bytes accessed | tf_op | source)
XLA Modules:
  0.0 1084.5 jit_solution(1804793181118891656)
XLA Ops:
  12.1 84.4 %all-gather.3.cloned.1.call-done = bf16[3,2048,256]{2,1,0:T(8,128)(2,1)} async-done(((bf16[3,32,256]{2,1,0:T(8,128)(2,1)}), bf16[3,2048,256]{2,1,0:T(8,128)(2,1)}) %all-gather.3.cloned.1.call-update) | async-done | bytes 3145744 | tf_op jit(solution)/shard_map/all_gather | solution.py:74
  96.5 67.6 %all-gather.5.cloned.1.call-done = bf16[1024,2048]{1,0:T(8,128)(2,1)} async-done(((bf16[1024,256]{1,0:T(8,128)(2,1)}), bf16[1024,2048]{1,0:T(8,128)(2,1)}) %all-gather.5.cloned.1.call-update) | async-done | bytes 4194320 | tf_op jit(solution)/shard_map/all_gather | solution.py:70
  164.0 6.6 fusion.15
  176.5 877.2 %while.28 = (s32[]{:T(128)}, bf16[2,128,128]{2,1,0:T(8,128)(2,1)S(1)}, bf16[]{:T(256)}, bf16[2,128,128]{2,1,0:T(8,128)(2,1)}, f32[]{:T(128)}, /*index=5*/f32[]{:...) while((s32[]{:T(128)}, bf16[2,128,128]{2,1,0:T(8,128)(2,1)S(1)}, bf16[]{:T(256)}, ...), condition=%wide.region_3.4_spmd, body=%wide.region_2.3_spmd.sunk | while | flops 163846 | bytes 590031 | solution.py:90
  195.3 5.4 collective-permute-done
  209.2 5.4 collective-permute-done
  223.1 5.4 collective-permute-done
  264.9 5.4 collective-permute-done
  278.8 5.4 collective-permute-done
  292.7 5.4 collective-permute-done
  306.6 5.4 collective-permute-done
  320.6 5.4 collective-permute-done
  334.5 5.4 collective-permute-done
  348.4 5.4 collective-permute-done
  362.3 5.4 collective-permute-done
  404.1 5.4 collective-permute-done
  418.0 5.4 collective-permute-done
  432.0 5.4 collective-permute-done
  445.9 5.4 collective-permute-done
  459.8 5.4 collective-permute-done
  473.7 5.4 collective-permute-done
  487.6 5.4 collective-permute-done
  529.4 5.4 collective-permute-done
  543.3 5.4 collective-permute-done
  557.3 5.4 collective-permute-done
  571.2 5.4 collective-permute-done
  585.1 5.4 collective-permute-done
  599.0 5.4 collective-permute-done
  613.0 5.4 collective-permute-done
  626.9 5.4 collective-permute-done
  668.6 5.4 collective-permute-done
  1056.0 19.2 %while.29 = (s32[]{:T(128)}, f32[2,512,2,128]{1,0,3,2:T(2,128)S(1)}, s32[2]{0:T(128)S(1)}, f32[1024]{0:T(1024)S(1)}, bf16[1024,2,128]{2,1,0:T(2,128)(2,1)S(1)}, ...) while((s32[]{:T(128)}, ...), condition=%wide.region_1.2_spmd.clone, body=%wide.region_0.1_spmd.clone.sunk | while | flops 540541440 | bytes 5519551 | solution.py:62
  (335 shorter events, 568.7 us)
Async XLA Ops:
  6.5 89.9 %all-gather.3.cloned.1.call-start = ((), (), s32[]{:S(2)}) async-start(), calls=%async_computation | async-start | bytes 3194880 | tf_op jit(solution)/shard_map/all_gather | solution.py:74
  7.3 156.8 %all-gather.5.cloned.1.call-start = ((), (), s32[]{:S(2)}) async-start(), calls=%async_computation.1 | async-start | bytes 4718592 | tf_op jit(solution)/shard_map/all_gather | solution.py:70
  176.5 13.3 %collective-permute-start.1 = (bf16[2,128,128]{2,1,0:T(8,128)(2,1)S(1)}, bf16[2,128,128]{2,1,0:T(8,128)(2,1)S(1)}, u32[]{:S(2)}, u32[]{:S(2)}) collective-permute-start(bf16[2,128,128]{2,1,0:T(8,128)(2,1)S(1)} %get-tuple-element.318), channel_id=1, source_target_pairs={{0,8},{8,16},{16,24},{24,32},{32,40},{40,48},{48,56},{56,64},{64,7... | collective-permute-start | bytes 196616 | tf_op jit(solution)/shard_map/while/body/eval_jaxpr/ppermute | solution.py:12
  190.5 13.3 %collective-permute-start.1 = (bf16[2,128,128]{2,1,0:T(8,128)(2,1)S(1)}, bf16[2,128,128]{2,1,0:T(8,128)(2,1)S(1)}, u32[]{:S(2)}, u32[]{:S(2)}) collective-permute-start(bf16[2,128,128]{2,1,0:T(8,128)(2,1)S(1)} %get-tuple-element.318), channel_id=1, source_target_pairs={{0,8},{8,16},{16,24},{24,32},{32,40},{40,48},{48,56},{56,64},{64,7... | collective-permute-start | bytes 196616 | tf_op jit(solution)/shard_map/while/body/eval_jaxpr/ppermute | solution.py:12
  204.4 13.3 %collective-permute-start.1 = (bf16[2,128,128]{2,1,0:T(8,128)(2,1)S(1)}, bf16[2,128,128]{2,1,0:T(8,128)(2,1)S(1)}, u32[]{:S(2)}, u32[]{:S(2)}) collective-permute-start(bf16[2,128,128]{2,1,0:T(8,128)(2,1)S(1)} %get-tuple-element.318), channel_id=1, source_target_pairs={{0,8},{8,16},{16,24},{24,32},{32,40},{40,48},{48,56},{56,64},{64,7... | collective-permute-start | bytes 196616 | tf_op jit(solution)/shard_map/while/body/eval_jaxpr/ppermute | solution.py:12
  218.3 13.3 %collective-permute-start.1 = (bf16[2,128,128]{2,1,0:T(8,128)(2,1)S(1)}, bf16[2,128,128]{2,1,0:T(8,128)(2,1)S(1)}, u32[]{:S(2)}, u32[]{:S(2)}) collective-permute-start(bf16[2,128,128]{2,1,0:T(8,128)(2,1)S(1)} %get-tuple-element.318), channel_id=1, source_target_pairs={{0,8},{8,16},{16,24},{24,32},{32,40},{40,48},{48,56},{56,64},{64,7... | collective-permute-start | bytes 196616 | tf_op jit(solution)/shard_map/while/body/eval_jaxpr/ppermute | solution.py:12
  287.9 13.3 %collective-permute-start.1 = (bf16[2,128,128]{2,1,0:T(8,128)(2,1)S(1)}, bf16[2,128,128]{2,1,0:T(8,128)(2,1)S(1)}, u32[]{:S(2)}, u32[]{:S(2)}) collective-permute-start(bf16[2,128,128]{2,1,0:T(8,128)(2,1)S(1)} %get-tuple-element.318), channel_id=1, source_target_pairs={{0,8},{8,16},{16,24},{24,32},{32,40},{40,48},{48,56},{56,64},{64,7... | collective-permute-start | bytes 196616 | tf_op jit(solution)/shard_map/while/body/eval_jaxpr/ppermute | solution.py:12
  301.9 13.3 %collective-permute-start.1 = (bf16[2,128,128]{2,1,0:T(8,128)(2,1)S(1)}, bf16[2,128,128]{2,1,0:T(8,128)(2,1)S(1)}, u32[]{:S(2)}, u32[]{:S(2)}) collective-permute-start(bf16[2,128,128]{2,1,0:T(8,128)(2,1)S(1)} %get-tuple-element.318), channel_id=1, source_target_pairs={{0,8},{8,16},{16,24},{24,32},{32,40},{40,48},{48,56},{56,64},{64,7... | collective-permute-start | bytes 196616 | tf_op jit(solution)/shard_map/while/body/eval_jaxpr/ppermute | solution.py:12
  315.8 13.3 %collective-permute-start.1 = (bf16[2,128,128]{2,1,0:T(8,128)(2,1)S(1)}, bf16[2,128,128]{2,1,0:T(8,128)(2,1)S(1)}, u32[]{:S(2)}, u32[]{:S(2)}) collective-permute-start(bf16[2,128,128]{2,1,0:T(8,128)(2,1)S(1)} %get-tuple-element.318), channel_id=1, source_target_pairs={{0,8},{8,16},{16,24},{24,32},{32,40},{40,48},{48,56},{56,64},{64,7... | collective-permute-start | bytes 196616 | tf_op jit(solution)/shard_map/while/body/eval_jaxpr/ppermute | solution.py:12
  329.7 13.3 %collective-permute-start.1 = (bf16[2,128,128]{2,1,0:T(8,128)(2,1)S(1)}, bf16[2,128,128]{2,1,0:T(8,128)(2,1)S(1)}, u32[]{:S(2)}, u32[]{:S(2)}) collective-permute-start(bf16[2,128,128]{2,1,0:T(8,128)(2,1)S(1)} %get-tuple-element.318), channel_id=1, source_target_pairs={{0,8},{8,16},{16,24},{24,32},{32,40},{40,48},{48,56},{56,64},{64,7... | collective-permute-start | bytes 196616 | tf_op jit(solution)/shard_map/while/body/eval_jaxpr/ppermute | solution.py:12
  343.6 13.3 %collective-permute-start.1 = (bf16[2,128,128]{2,1,0:T(8,128)(2,1)S(1)}, bf16[2,128,128]{2,1,0:T(8,128)(2,1)S(1)}, u32[]{:S(2)}, u32[]{:S(2)}) collective-permute-start(bf16[2,128,128]{2,1,0:T(8,128)(2,1)S(1)} %get-tuple-element.318), channel_id=1, source_target_pairs={{0,8},{8,16},{16,24},{24,32},{32,40},{40,48},{48,56},{56,64},{64,7... | collective-permute-start | bytes 196616 | tf_op jit(solution)/shard_map/while/body/eval_jaxpr/ppermute | solution.py:12
  413.3 13.3 %collective-permute-start.1 = (bf16[2,128,128]{2,1,0:T(8,128)(2,1)S(1)}, bf16[2,128,128]{2,1,0:T(8,128)(2,1)S(1)}, u32[]{:S(2)}, u32[]{:S(2)}) collective-permute-start(bf16[2,128,128]{2,1,0:T(8,128)(2,1)S(1)} %get-tuple-element.318), channel_id=1, source_target_pairs={{0,8},{8,16},{16,24},{24,32},{32,40},{40,48},{48,56},{56,64},{64,7... | collective-permute-start | bytes 196616 | tf_op jit(solution)/shard_map/while/body/eval_jaxpr/ppermute | solution.py:12
  427.2 13.3 %collective-permute-start.1 = (bf16[2,128,128]{2,1,0:T(8,128)(2,1)S(1)}, bf16[2,128,128]{2,1,0:T(8,128)(2,1)S(1)}, u32[]{:S(2)}, u32[]{:S(2)}) collective-permute-start(bf16[2,128,128]{2,1,0:T(8,128)(2,1)S(1)} %get-tuple-element.318), channel_id=1, source_target_pairs={{0,8},{8,16},{16,24},{24,32},{32,40},{40,48},{48,56},{56,64},{64,7... | collective-permute-start | bytes 196616 | tf_op jit(solution)/shard_map/while/body/eval_jaxpr/ppermute | solution.py:12
  441.1 13.3 %collective-permute-start.1 = (bf16[2,128,128]{2,1,0:T(8,128)(2,1)S(1)}, bf16[2,128,128]{2,1,0:T(8,128)(2,1)S(1)}, u32[]{:S(2)}, u32[]{:S(2)}) collective-permute-start(bf16[2,128,128]{2,1,0:T(8,128)(2,1)S(1)} %get-tuple-element.318), channel_id=1, source_target_pairs={{0,8},{8,16},{16,24},{24,32},{32,40},{40,48},{48,56},{56,64},{64,7... | collective-permute-start | bytes 196616 | tf_op jit(solution)/shard_map/while/body/eval_jaxpr/ppermute | solution.py:12
  455.0 13.3 %collective-permute-start.1 = (bf16[2,128,128]{2,1,0:T(8,128)(2,1)S(1)}, bf16[2,128,128]{2,1,0:T(8,128)(2,1)S(1)}, u32[]{:S(2)}, u32[]{:S(2)}) collective-permute-start(bf16[2,128,128]{2,1,0:T(8,128)(2,1)S(1)} %get-tuple-element.318), channel_id=1, source_target_pairs={{0,8},{8,16},{16,24},{24,32},{32,40},{40,48},{48,56},{56,64},{64,7... | collective-permute-start | bytes 196616 | tf_op jit(solution)/shard_map/while/body/eval_jaxpr/ppermute | solution.py:12
  468.9 13.3 %collective-permute-start.1 = (bf16[2,128,128]{2,1,0:T(8,128)(2,1)S(1)}, bf16[2,128,128]{2,1,0:T(8,128)(2,1)S(1)}, u32[]{:S(2)}, u32[]{:S(2)}) collective-permute-start(bf16[2,128,128]{2,1,0:T(8,128)(2,1)S(1)} %get-tuple-element.318), channel_id=1, source_target_pairs={{0,8},{8,16},{16,24},{24,32},{32,40},{40,48},{48,56},{56,64},{64,7... | collective-permute-start | bytes 196616 | tf_op jit(solution)/shard_map/while/body/eval_jaxpr/ppermute | solution.py:12
  482.9 13.3 %collective-permute-start.1 = (bf16[2,128,128]{2,1,0:T(8,128)(2,1)S(1)}, bf16[2,128,128]{2,1,0:T(8,128)(2,1)S(1)}, u32[]{:S(2)}, u32[]{:S(2)}) collective-permute-start(bf16[2,128,128]{2,1,0:T(8,128)(2,1)S(1)} %get-tuple-element.318), channel_id=1, source_target_pairs={{0,8},{8,16},{16,24},{24,32},{32,40},{40,48},{48,56},{56,64},{64,7... | collective-permute-start | bytes 196616 | tf_op jit(solution)/shard_map/while/body/eval_jaxpr/ppermute | solution.py:12
  552.5 13.3 %collective-permute-start.1 = (bf16[2,128,128]{2,1,0:T(8,128)(2,1)S(1)}, bf16[2,128,128]{2,1,0:T(8,128)(2,1)S(1)}, u32[]{:S(2)}, u32[]{:S(2)}) collective-permute-start(bf16[2,128,128]{2,1,0:T(8,128)(2,1)S(1)} %get-tuple-element.318), channel_id=1, source_target_pairs={{0,8},{8,16},{16,24},{24,32},{32,40},{40,48},{48,56},{56,64},{64,7... | collective-permute-start | bytes 196616 | tf_op jit(solution)/shard_map/while/body/eval_jaxpr/ppermute | solution.py:12
  566.4 13.3 %collective-permute-start.1 = (bf16[2,128,128]{2,1,0:T(8,128)(2,1)S(1)}, bf16[2,128,128]{2,1,0:T(8,128)(2,1)S(1)}, u32[]{:S(2)}, u32[]{:S(2)}) collective-permute-start(bf16[2,128,128]{2,1,0:T(8,128)(2,1)S(1)} %get-tuple-element.318), channel_id=1, source_target_pairs={{0,8},{8,16},{16,24},{24,32},{32,40},{40,48},{48,56},{56,64},{64,7... | collective-permute-start | bytes 196616 | tf_op jit(solution)/shard_map/while/body/eval_jaxpr/ppermute | solution.py:12
  580.3 13.3 %collective-permute-start.1 = (bf16[2,128,128]{2,1,0:T(8,128)(2,1)S(1)}, bf16[2,128,128]{2,1,0:T(8,128)(2,1)S(1)}, u32[]{:S(2)}, u32[]{:S(2)}) collective-permute-start(bf16[2,128,128]{2,1,0:T(8,128)(2,1)S(1)} %get-tuple-element.318), channel_id=1, source_target_pairs={{0,8},{8,16},{16,24},{24,32},{32,40},{40,48},{48,56},{56,64},{64,7... | collective-permute-start | bytes 196616 | tf_op jit(solution)/shard_map/while/body/eval_jaxpr/ppermute | solution.py:12
  594.3 13.3 %collective-permute-start.1 = (bf16[2,128,128]{2,1,0:T(8,128)(2,1)S(1)}, bf16[2,128,128]{2,1,0:T(8,128)(2,1)S(1)}, u32[]{:S(2)}, u32[]{:S(2)}) collective-permute-start(bf16[2,128,128]{2,1,0:T(8,128)(2,1)S(1)} %get-tuple-element.318), channel_id=1, source_target_pairs={{0,8},{8,16},{16,24},{24,32},{32,40},{40,48},{48,56},{56,64},{64,7... | collective-permute-start | bytes 196616 | tf_op jit(solution)/shard_map/while/body/eval_jaxpr/ppermute | solution.py:12
  608.2 13.3 %collective-permute-start.1 = (bf16[2,128,128]{2,1,0:T(8,128)(2,1)S(1)}, bf16[2,128,128]{2,1,0:T(8,128)(2,1)S(1)}, u32[]{:S(2)}, u32[]{:S(2)}) collective-permute-start(bf16[2,128,128]{2,1,0:T(8,128)(2,1)S(1)} %get-tuple-element.318), channel_id=1, source_target_pairs={{0,8},{8,16},{16,24},{24,32},{32,40},{40,48},{48,56},{56,64},{64,7... | collective-permute-start | bytes 196616 | tf_op jit(solution)/shard_map/while/body/eval_jaxpr/ppermute | solution.py:12
  677.8 13.3 %collective-permute-start.1 = (bf16[2,128,128]{2,1,0:T(8,128)(2,1)S(1)}, bf16[2,128,128]{2,1,0:T(8,128)(2,1)S(1)}, u32[]{:S(2)}, u32[]{:S(2)}) collective-permute-start(bf16[2,128,128]{2,1,0:T(8,128)(2,1)S(1)} %get-tuple-element.318), channel_id=1, source_target_pairs={{0,8},{8,16},{16,24},{24,32},{32,40},{40,48},{48,56},{56,64},{64,7... | collective-permute-start | bytes 196616 | tf_op jit(solution)/shard_map/while/body/eval_jaxpr/ppermute | solution.py:12
  691.7 13.3 %collective-permute-start.1 = (bf16[2,128,128]{2,1,0:T(8,128)(2,1)S(1)}, bf16[2,128,128]{2,1,0:T(8,128)(2,1)S(1)}, u32[]{:S(2)}, u32[]{:S(2)}) collective-permute-start(bf16[2,128,128]{2,1,0:T(8,128)(2,1)S(1)} %get-tuple-element.318), channel_id=1, source_target_pairs={{0,8},{8,16},{16,24},{24,32},{32,40},{40,48},{48,56},{56,64},{64,7... | collective-permute-start | bytes 196616 | tf_op jit(solution)/shard_map/while/body/eval_jaxpr/ppermute | solution.py:12
  705.6 13.3 %collective-permute-start.1 = (bf16[2,128,128]{2,1,0:T(8,128)(2,1)S(1)}, bf16[2,128,128]{2,1,0:T(8,128)(2,1)S(1)}, u32[]{:S(2)}, u32[]{:S(2)}) collective-permute-start(bf16[2,128,128]{2,1,0:T(8,128)(2,1)S(1)} %get-tuple-element.318), channel_id=1, source_target_pairs={{0,8},{8,16},{16,24},{24,32},{32,40},{40,48},{48,56},{56,64},{64,7... | collective-permute-start | bytes 196616 | tf_op jit(solution)/shard_map/while/body/eval_jaxpr/ppermute | solution.py:12
  719.6 13.3 %collective-permute-start.1 = (bf16[2,128,128]{2,1,0:T(8,128)(2,1)S(1)}, bf16[2,128,128]{2,1,0:T(8,128)(2,1)S(1)}, u32[]{:S(2)}, u32[]{:S(2)}) collective-permute-start(bf16[2,128,128]{2,1,0:T(8,128)(2,1)S(1)} %get-tuple-element.318), channel_id=1, source_target_pairs={{0,8},{8,16},{16,24},{24,32},{32,40},{40,48},{48,56},{56,64},{64,7... | collective-permute-start | bytes 196616 | tf_op jit(solution)/shard_map/while/body/eval_jaxpr/ppermute | solution.py:12
  733.5 13.3 %collective-permute-start.1 = (bf16[2,128,128]{2,1,0:T(8,128)(2,1)S(1)}, bf16[2,128,128]{2,1,0:T(8,128)(2,1)S(1)}, u32[]{:S(2)}, u32[]{:S(2)}) collective-permute-start(bf16[2,128,128]{2,1,0:T(8,128)(2,1)S(1)} %get-tuple-element.318), channel_id=1, source_target_pairs={{0,8},{8,16},{16,24},{24,32},{32,40},{40,48},{48,56},{56,64},{64,7... | collective-permute-start | bytes 196616 | tf_op jit(solution)/shard_map/while/body/eval_jaxpr/ppermute | solution.py:12
  747.4 13.3 %collective-permute-start.1 = (bf16[2,128,128]{2,1,0:T(8,128)(2,1)S(1)}, bf16[2,128,128]{2,1,0:T(8,128)(2,1)S(1)}, u32[]{:S(2)}, u32[]{:S(2)}) collective-permute-start(bf16[2,128,128]{2,1,0:T(8,128)(2,1)S(1)} %get-tuple-element.318), channel_id=1, source_target_pairs={{0,8},{8,16},{16,24},{24,32},{32,40},{40,48},{48,56},{56,64},{64,7... | collective-permute-start | bytes 196616 | tf_op jit(solution)/shard_map/while/body/eval_jaxpr/ppermute | solution.py:12
  817.0 13.3 %collective-permute-start.1 = (bf16[2,128,128]{2,1,0:T(8,128)(2,1)S(1)}, bf16[2,128,128]{2,1,0:T(8,128)(2,1)S(1)}, u32[]{:S(2)}, u32[]{:S(2)}) collective-permute-start(bf16[2,128,128]{2,1,0:T(8,128)(2,1)S(1)} %get-tuple-element.318), channel_id=1, source_target_pairs={{0,8},{8,16},{16,24},{24,32},{32,40},{40,48},{48,56},{56,64},{64,7... | collective-permute-start | bytes 196616 | tf_op jit(solution)/shard_map/while/body/eval_jaxpr/ppermute | solution.py:12
  830.9 13.3 %collective-permute-start.1 = (bf16[2,128,128]{2,1,0:T(8,128)(2,1)S(1)}, bf16[2,128,128]{2,1,0:T(8,128)(2,1)S(1)}, u32[]{:S(2)}, u32[]{:S(2)}) collective-permute-start(bf16[2,128,128]{2,1,0:T(8,128)(2,1)S(1)} %get-tuple-element.318), channel_id=1, source_target_pairs={{0,8},{8,16},{16,24},{24,32},{32,40},{40,48},{48,56},{56,64},{64,7... | collective-permute-start | bytes 196616 | tf_op jit(solution)/shard_map/while/body/eval_jaxpr/ppermute | solution.py:12
  844.9 13.3 %collective-permute-start.1 = (bf16[2,128,128]{2,1,0:T(8,128)(2,1)S(1)}, bf16[2,128,128]{2,1,0:T(8,128)(2,1)S(1)}, u32[]{:S(2)}, u32[]{:S(2)}) collective-permute-start(bf16[2,128,128]{2,1,0:T(8,128)(2,1)S(1)} %get-tuple-element.318), channel_id=1, source_target_pairs={{0,8},{8,16},{16,24},{24,32},{32,40},{40,48},{48,56},{56,64},{64,7... | collective-permute-start | bytes 196616 | tf_op jit(solution)/shard_map/while/body/eval_jaxpr/ppermute | solution.py:12
  858.8 13.3 %collective-permute-start.1 = (bf16[2,128,128]{2,1,0:T(8,128)(2,1)S(1)}, bf16[2,128,128]{2,1,0:T(8,128)(2,1)S(1)}, u32[]{:S(2)}, u32[]{:S(2)}) collective-permute-start(bf16[2,128,128]{2,1,0:T(8,128)(2,1)S(1)} %get-tuple-element.318), channel_id=1, source_target_pairs={{0,8},{8,16},{16,24},{24,32},{32,40},{40,48},{48,56},{56,64},{64,7... | collective-permute-start | bytes 196616 | tf_op jit(solution)/shard_map/while/body/eval_jaxpr/ppermute | solution.py:12
  (100 other events, 2743.7 us)
Sparse Core Ops, SparseCore 0:
  10.8 85.6 all-gather.2
  98.5 65.5 all-gather.4
where the time goes:
time: 1090 us; the launch traced here: 1080 us
  waiting for transfers between devices  494 us (45%)
  starting transfers between devices  302 us (28%)
  loops' own time  196 us (18%)
  other arithmetic  50.1 us (5%)
  local copies, waits for them, and re-layouts  16.1 us (1%)
  between operations  14.9 us (1%)
  matrix products  11.9 us (1%)
    ppermute x126, waiting for transfers between devices, passed_along(): lax.ppermute(value, axis, [(source, source + steps) for source in range(l...  340 us
    ppermute x126, starting transfers between devices, passed_along(): lax.ppermute(value, axis, [(source, source + steps) for source in range(l...  302 us
    another operation x1, loops' own time, per_device(): lax.fori_loop(0, lax.axis_size('ctx') - 1, hand_round, (own_pair, start_p...  194 us
    all_gather x1, waiting for transfers between devices, per_device(): lax.all_gather(w_qkv, 'ctx', axis=1, tiled=True)  84.4 us
    all_gather x1, waiting for transfers between devices, per_device(): whole = lax.all_gather(tokens, 'head', axis=1, tiled=True)  67.6 us
    add x63, other arithmetic, combine(): later_state + jnp.where(linked, first_state, 0.0)  40.5 us
  transfers between devices with their start and end apart: 128, of which 65 were waited for; matrix products, arithmetic and copies ran while one was open for 0% of the time, Pallas kernels for 0%

commit v1 on v0

--- a/solution.py
+++ b/solution.py
@@ -71,7 +71,9 @@
     projected = jnp.einsum(
         "tr,grc->gtc",
         whole,
-        lax.all_gather(w_qkv, "ctx", axis=1, tiled=True),
+        jnp.concatenate(
+            lax.all_to_all(jnp.stack(lax.axis_size("ctx") * [w_qkv]), "ctx", 0, 0), axis=1
+        ),
         preferred_element_type=jnp.float32,
     ).astype(jnp.bfloat16)
     queries, key_map, values, seg_float, kv_state, tail_id = prepare(projected, seg_ids)

time: 1090 us -> 1010 us (0.927)
  the two profiles are of different devices: /device:TPU:32 before, /device:TPU:480 now
where the time goes in v1:
time: 1010 us; the launch traced here: 1000 us
  waiting for transfers between devices  410 us (41%)
  starting transfers between devices  311 us (31%)
  loops' own time  190 us (19%)
  other arithmetic  42.9 us (4%)
  local copies, waits for them, and re-layouts  21 us (2%)
  between operations  14.7 us (1%)
  matrix products  12.1 us (1%)
    ppermute x126, waiting for transfers between devices, passed_along(): lax.ppermute(value, axis, [(source, source + steps) for source in range(l...  342 us
    ppermute x126, starting transfers between devices, passed_along(): lax.ppermute(value, axis, [(source, source + steps) for source in range(l...  300 us
    another operation x1, loops' own time, per_device(): lax.fori_loop(0, lax.axis_size('ctx') - 1, hand_round, (own_pair, start_p...  189 us
    all_to_all x1, waiting for transfers between devices, per_device(): lax.all_to_all(jnp.stack(lax.axis_size('ctx') * [w_qkv]), 'ctx', 0, 0)  67.3 us
    add x63, other arithmetic, combine(): later_state + jnp.where(linked, first_state, 0.0)  40.3 us
  transfers between devices with their start and end apart: 128, of which 64 were waited for; matrix products, arithmetic and copies ran while one was open for 1% of the time, Pallas kernels for 0%

profile of v1, /device:TPU:480, one launch (start us, length us, event | category | flops | bytes accessed | tf_op | source)
XLA Modules:
  0.0 1001.6 jit_solution(8587329449426272899)
XLA Ops:
  10.2 10.5 %all-to-all-start = ((bf16[64,3,32,256]{3,2,1,0:T(8,128)(2,1)}), bf16[64,3,32,256]{3,2,1,0:T(8,128)(2,1)S(1)}, u32[]{:S(2)}, u32[]{:S(2)}) async-start(bf16[64,3,32,256]{3,2,1,0:T(8,128)(2,1)} %stack.2), calls=%async_computation | async-start | bytes 6291456 | tf_op jit(solution)/shard_map/all_to_all | solution.py:75
  22.9 67.3 %all-to-all-done = bf16[64,3,32,256]{3,2,1,0:T(8,128)(2,1)S(1)} async-done(((bf16[64,3,32,256]{3,2,1,0:T(8,128)(2,1)}), bf16[64,3,32,256]{3,2,1,0:T(8,128)(2,1)S(1)}, u32[]{:S(2)}, u32[]{:S(2)}) %all-to-all-start) | async-done | bytes 3145760 | tf_op jit(solution)/shard_map/all_to_all | solution.py:75
  92.3 6.6 fusion.15
  102.2 871.6 %while.28 = (s32[]{:T(128)}, bf16[2,128,128]{2,1,0:T(8,128)(2,1)S(1)}, bf16[]{:T(256)}, bf16[2,128,128]{2,1,0:T(8,128)(2,1)}, f32[]{:T(128)}, /*index=5*/f32[]{:...) while((s32[]{:T(128)}, bf16[2,128,128]{2,1,0:T(8,128)(2,1)S(1)}, bf16[]{:T(256)}, ...), condition=%wide.region_3.4_spmd, body=%wide.region_2.3_spmd.sunk | while | flops 163846 | bytes 590031 | solution.py:92
  120.8 5.4 collective-permute-done
  134.6 5.4 collective-permute-done
  148.4 5.4 collective-permute-done
  162.3 5.4 collective-permute-done
  176.1 5.4 collective-permute-done
  189.9 5.4 collective-permute-done
  217.6 5.4 collective-permute-done
  245.3 5.4 collective-permute-done
  272.9 5.4 collective-permute-done
  300.6 5.4 collective-permute-done
  314.4 5.4 collective-permute-done
  328.3 5.4 collective-permute-done
  342.1 5.4 collective-permute-done
  355.9 5.4 collective-permute-done
  369.8 5.4 collective-permute-done
  383.6 5.4 collective-permute-done
  397.4 5.4 collective-permute-done
  411.3 5.4 collective-permute-done
  425.1 5.4 collective-permute-done
  439.0 5.4 collective-permute-done
  452.8 5.4 collective-permute-done
  480.5 5.4 collective-permute-done
  508.1 5.4 collective-permute-done
  535.8 5.4 collective-permute-done
  563.5 5.4 collective-permute-done
  577.3 5.4 collective-permute-done
  591.1 5.4 collective-permute-done
  973.7 18.5 %while.29 = (s32[]{:T(128)}, f32[2,512,2,128]{1,0,3,2:T(2,128)S(1)}, s32[2]{0:T(128)S(1)}, f32[1024]{0:T(1024)S(1)}, bf16[1024,2,128]{2,0,1:T(8,128)(2,1)S(1)}, ...) while((s32[]{:T(128)}, ...), condition=%wide.region_1.2_spmd.clone, body=%wide.region_0.1_spmd.clone.sunk | while | flops 540541440 | bytes 4995255 | solution.py:62
  (337 shorter events, 565.8 us)
Async XLA Ops:
  6.5 85.8 %all-gather.2.cloned.1.call-start = ((), (), s32[]{:S(2)}) async-start(), calls=%async_computation.1 | async-start | bytes 4718592 | tf_op jit(solution)/shard_map/all_gather | solution.py:70
  10.2 80.1 %all-to-all-start = ((bf16[64,3,32,256]{3,2,1,0:T(8,128)(2,1)}), bf16[64,3,32,256]{3,2,1,0:T(8,128)(2,1)S(1)}, u32[]{:S(2)}, u32[]{:S(2)}) async-start(bf16[64,3,32,256]{3,2,1,0:T(8,128)(2,1)} %stack.2), calls=%async_computation | async-start | bytes 6291456 | tf_op jit(solution)/shard_map/all_to_all | solution.py:75
  102.2 13.2 %collective-permute-start.1 = (bf16[2,128,128]{2,1,0:T(8,128)(2,1)S(1)}, bf16[2,128,128]{2,1,0:T(8,128)(2,1)S(1)}, u32[]{:S(2)}, u32[]{:S(2)}) collective-permute-start(bf16[2,128,128]{2,1,0:T(8,128)(2,1)S(1)} %get-tuple-element.332), channel_id=1, source_target_pairs={{0,8},{8,16},{16,24},{24,32},{32,40},{40,48},{48,56},{56,64},{64,7... | collective-permute-start | bytes 196616 | tf_op jit(solution)/shard_map/while/body/eval_jaxpr/ppermute | solution.py:12
  116.0 13.2 %collective-permute-start.1 = (bf16[2,128,128]{2,1,0:T(8,128)(2,1)S(1)}, bf16[2,128,128]{2,1,0:T(8,128)(2,1)S(1)}, u32[]{:S(2)}, u32[]{:S(2)}) collective-permute-start(bf16[2,128,128]{2,1,0:T(8,128)(2,1)S(1)} %get-tuple-element.332), channel_id=1, source_target_pairs={{0,8},{8,16},{16,24},{24,32},{32,40},{40,48},{48,56},{56,64},{64,7... | collective-permute-start | bytes 196616 | tf_op jit(solution)/shard_map/while/body/eval_jaxpr/ppermute | solution.py:12
  129.8 13.2 %collective-permute-start.1 = (bf16[2,128,128]{2,1,0:T(8,128)(2,1)S(1)}, bf16[2,128,128]{2,1,0:T(8,128)(2,1)S(1)}, u32[]{:S(2)}, u32[]{:S(2)}) collective-permute-start(bf16[2,128,128]{2,1,0:T(8,128)(2,1)S(1)} %get-tuple-element.332), channel_id=1, source_target_pairs={{0,8},{8,16},{16,24},{24,32},{32,40},{40,48},{48,56},{56,64},{64,7... | collective-permute-start | bytes 196616 | tf_op jit(solution)/shard_map/while/body/eval_jaxpr/ppermute | solution.py:12
  143.7 13.2 %collective-permute-start.1 = (bf16[2,128,128]{2,1,0:T(8,128)(2,1)S(1)}, bf16[2,128,128]{2,1,0:T(8,128)(2,1)S(1)}, u32[]{:S(2)}, u32[]{:S(2)}) collective-permute-start(bf16[2,128,128]{2,1,0:T(8,128)(2,1)S(1)} %get-tuple-element.332), channel_id=1, source_target_pairs={{0,8},{8,16},{16,24},{24,32},{32,40},{40,48},{48,56},{56,64},{64,7... | collective-permute-start | bytes 196616 | tf_op jit(solution)/shard_map/while/body/eval_jaxpr/ppermute | solution.py:12
  157.5 13.2 %collective-permute-start.1 = (bf16[2,128,128]{2,1,0:T(8,128)(2,1)S(1)}, bf16[2,128,128]{2,1,0:T(8,128)(2,1)S(1)}, u32[]{:S(2)}, u32[]{:S(2)}) collective-permute-start(bf16[2,128,128]{2,1,0:T(8,128)(2,1)S(1)} %get-tuple-element.332), channel_id=1, source_target_pairs={{0,8},{8,16},{16,24},{24,32},{32,40},{40,48},{48,56},{56,64},{64,7... | collective-permute-start | bytes 196616 | tf_op jit(solution)/shard_map/while/body/eval_jaxpr/ppermute | solution.py:12
  171.3 13.2 %collective-permute-start.1 = (bf16[2,128,128]{2,1,0:T(8,128)(2,1)S(1)}, bf16[2,128,128]{2,1,0:T(8,128)(2,1)S(1)}, u32[]{:S(2)}, u32[]{:S(2)}) collective-permute-start(bf16[2,128,128]{2,1,0:T(8,128)(2,1)S(1)} %get-tuple-element.332), channel_id=1, source_target_pairs={{0,8},{8,16},{16,24},{24,32},{32,40},{40,48},{48,56},{56,64},{64,7... | collective-permute-start | bytes 196616 | tf_op jit(solution)/shard_map/while/body/eval_jaxpr/ppermute | solution.py:12
  185.2 13.2 %collective-permute-start.1 = (bf16[2,128,128]{2,1,0:T(8,128)(2,1)S(1)}, bf16[2,128,128]{2,1,0:T(8,128)(2,1)S(1)}, u32[]{:S(2)}, u32[]{:S(2)}) collective-permute-start(bf16[2,128,128]{2,1,0:T(8,128)(2,1)S(1)} %get-tuple-element.332), channel_id=1, source_target_pairs={{0,8},{8,16},{16,24},{24,32},{32,40},{40,48},{48,56},{56,64},{64,7... | collective-permute-start | bytes 196616 | tf_op jit(solution)/shard_map/while/body/eval_jaxpr/ppermute | solution.py:12
  199.0 13.2 %collective-permute-start.1 = (bf16[2,128,128]{2,1,0:T(8,128)(2,1)S(1)}, bf16[2,128,128]{2,1,0:T(8,128)(2,1)S(1)}, u32[]{:S(2)}, u32[]{:S(2)}) collective-permute-start(bf16[2,128,128]{2,1,0:T(8,128)(2,1)S(1)} %get-tuple-element.332), channel_id=1, source_target_pairs={{0,8},{8,16},{16,24},{24,32},{32,40},{40,48},{48,56},{56,64},{64,7... | collective-permute-start | bytes 196616 | tf_op jit(solution)/shard_map/while/body/eval_jaxpr/ppermute | solution.py:12
  212.8 13.2 %collective-permute-start.1 = (bf16[2,128,128]{2,1,0:T(8,128)(2,1)S(1)}, bf16[2,128,128]{2,1,0:T(8,128)(2,1)S(1)}, u32[]{:S(2)}, u32[]{:S(2)}) collective-permute-start(bf16[2,128,128]{2,1,0:T(8,128)(2,1)S(1)} %get-tuple-element.332), channel_id=1, source_target_pairs={{0,8},{8,16},{16,24},{24,32},{32,40},{40,48},{48,56},{56,64},{64,7... | collective-permute-start | bytes 196616 | tf_op jit(solution)/shard_map/while/body/eval_jaxpr/ppermute | solution.py:12
  226.7 13.2 %collective-permute-start.1 = (bf16[2,128,128]{2,1,0:T(8,128)(2,1)S(1)}, bf16[2,128,128]{2,1,0:T(8,128)(2,1)S(1)}, u32[]{:S(2)}, u32[]{:S(2)}) collective-permute-start(bf16[2,128,128]{2,1,0:T(8,128)(2,1)S(1)} %get-tuple-element.332), channel_id=1, source_target_pairs={{0,8},{8,16},{16,24},{24,32},{32,40},{40,48},{48,56},{56,64},{64,7... | collective-permute-start | bytes 196616 | tf_op jit(solution)/shard_map/while/body/eval_jaxpr/ppermute | solution.py:12
  240.5 13.2 %collective-permute-start.1 = (bf16[2,128,128]{2,1,0:T(8,128)(2,1)S(1)}, bf16[2,128,128]{2,1,0:T(8,128)(2,1)S(1)}, u32[]{:S(2)}, u32[]{:S(2)}) collective-permute-start(bf16[2,128,128]{2,1,0:T(8,128)(2,1)S(1)} %get-tuple-element.332), channel_id=1, source_target_pairs={{0,8},{8,16},{16,24},{24,32},{32,40},{40,48},{48,56},{56,64},{64,7... | collective-permute-start | bytes 196616 | tf_op jit(solution)/shard_map/while/body/eval_jaxpr/ppermute | solution.py:12
  254.3 13.2 %collective-permute-start.1 = (bf16[2,128,128]{2,1,0:T(8,128)(2,1)S(1)}, bf16[2,128,128]{2,1,0:T(8,128)(2,1)S(1)}, u32[]{:S(2)}, u32[]{:S(2)}) collective-permute-start(bf16[2,128,128]{2,1,0:T(8,128)(2,1)S(1)} %get-tuple-element.332), channel_id=1, source_target_pairs={{0,8},{8,16},{16,24},{24,32},{32,40},{40,48},{48,56},{56,64},{64,7... | collective-permute-start | bytes 196616 | tf_op jit(solution)/shard_map/while/body/eval_jaxpr/ppermute | solution.py:12
  268.2 13.2 %collective-permute-start.1 = (bf16[2,128,128]{2,1,0:T(8,128)(2,1)S(1)}, bf16[2,128,128]{2,1,0:T(8,128)(2,1)S(1)}, u32[]{:S(2)}, u32[]{:S(2)}) collective-permute-start(bf16[2,128,128]{2,1,0:T(8,128)(2,1)S(1)} %get-tuple-element.332), channel_id=1, source_target_pairs={{0,8},{8,16},{16,24},{24,32},{32,40},{40,48},{48,56},{56,64},{64,7... | collective-permute-start | bytes 196616 | tf_op jit(solution)/shard_map/while/body/eval_jaxpr/ppermute | solution.py:12
  282.0 13.2 %collective-permute-start.1 = (bf16[2,128,128]{2,1,0:T(8,128)(2,1)S(1)}, bf16[2,128,128]{2,1,0:T(8,128)(2,1)S(1)}, u32[]{:S(2)}, u32[]{:S(2)}) collective-permute-start(bf16[2,128,128]{2,1,0:T(8,128)(2,1)S(1)} %get-tuple-element.332), channel_id=1, source_target_pairs={{0,8},{8,16},{16,24},{24,32},{32,40},{40,48},{48,56},{56,64},{64,7... | collective-permute-start | bytes 196616 | tf_op jit(solution)/shard_map/while/body/eval_jaxpr/ppermute | solution.py:12
  295.8 13.2 %collective-permute-start.1 = (bf16[2,128,128]{2,1,0:T(8,128)(2,1)S(1)}, bf16[2,128,128]{2,1,0:T(8,128)(2,1)S(1)}, u32[]{:S(2)}, u32[]{:S(2)}) collective-permute-start(bf16[2,128,128]{2,1,0:T(8,128)(2,1)S(1)} %get-tuple-element.332), channel_id=1, source_target_pairs={{0,8},{8,16},{16,24},{24,32},{32,40},{40,48},{48,56},{56,64},{64,7... | collective-permute-start | bytes 196616 | tf_op jit(solution)/shard_map/while/body/eval_jaxpr/ppermute | solution.py:12
  309.7 13.2 %collective-permute-start.1 = (bf16[2,128,128]{2,1,0:T(8,128)(2,1)S(1)}, bf16[2,128,128]{2,1,0:T(8,128)(2,1)S(1)}, u32[]{:S(2)}, u32[]{:S(2)}) collective-permute-start(bf16[2,128,128]{2,1,0:T(8,128)(2,1)S(1)} %get-tuple-element.332), channel_id=1, source_target_pairs={{0,8},{8,16},{16,24},{24,32},{32,40},{40,48},{48,56},{56,64},{64,7... | collective-permute-start | bytes 196616 | tf_op jit(solution)/shard_map/while/body/eval_jaxpr/ppermute | solution.py:12
  323.5 13.2 %collective-permute-start.1 = (bf16[2,128,128]{2,1,0:T(8,128)(2,1)S(1)}, bf16[2,128,128]{2,1,0:T(8,128)(2,1)S(1)}, u32[]{:S(2)}, u32[]{:S(2)}) collective-permute-start(bf16[2,128,128]{2,1,0:T(8,128)(2,1)S(1)} %get-tuple-element.332), channel_id=1, source_target_pairs={{0,8},{8,16},{16,24},{24,32},{32,40},{40,48},{48,56},{56,64},{64,7... | collective-permute-start | bytes 196616 | tf_op jit(solution)/shard_map/while/body/eval_jaxpr/ppermute | solution.py:12
  337.3 13.2 %collective-permute-start.1 = (bf16[2,128,128]{2,1,0:T(8,128)(2,1)S(1)}, bf16[2,128,128]{2,1,0:T(8,128)(2,1)S(1)}, u32[]{:S(2)}, u32[]{:S(2)}) collective-permute-start(bf16[2,128,128]{2,1,0:T(8,128)(2,1)S(1)} %get-tuple-element.332), channel_id=1, source_target_pairs={{0,8},{8,16},{16,24},{24,32},{32,40},{40,48},{48,56},{56,64},{64,7... | collective-permute-start | bytes 196616 | tf_op jit(solution)/shard_map/while/body/eval_jaxpr/ppermute | solution.py:12
  351.2 13.2 %collective-permute-start.1 = (bf16[2,128,128]{2,1,0:T(8,128)(2,1)S(1)}, bf16[2,128,128]{2,1,0:T(8,128)(2,1)S(1)}, u32[]{:S(2)}, u32[]{:S(2)}) collective-permute-start(bf16[2,128,128]{2,1,0:T(8,128)(2,1)S(1)} %get-tuple-element.332), channel_id=1, source_target_pairs={{0,8},{8,16},{16,24},{24,32},{32,40},{40,48},{48,56},{56,64},{64,7... | collective-permute-start | bytes 196616 | tf_op jit(solution)/shard_map/while/body/eval_jaxpr/ppermute | solution.py:12
  365.0 13.2 %collective-permute-start.1 = (bf16[2,128,128]{2,1,0:T(8,128)(2,1)S(1)}, bf16[2,128,128]{2,1,0:T(8,128)(2,1)S(1)}, u32[]{:S(2)}, u32[]{:S(2)}) collective-permute-start(bf16[2,128,128]{2,1,0:T(8,128)(2,1)S(1)} %get-tuple-element.332), channel_id=1, source_target_pairs={{0,8},{8,16},{16,24},{24,32},{32,40},{40,48},{48,56},{56,64},{64,7... | collective-permute-start | bytes 196616 | tf_op jit(solution)/shard_map/while/body/eval_jaxpr/ppermute | solution.py:12
  378.8 13.2 %collective-permute-start.1 = (bf16[2,128,128]{2,1,0:T(8,128)(2,1)S(1)}, bf16[2,128,128]{2,1,0:T(8,128)(2,1)S(1)}, u32[]{:S(2)}, u32[]{:S(2)}) collective-permute-start(bf16[2,128,128]{2,1,0:T(8,128)(2,1)S(1)} %get-tuple-element.332), channel_id=1, source_target_pairs={{0,8},{8,16},{16,24},{24,32},{32,40},{40,48},{48,56},{56,64},{64,7... | collective-permute-start | bytes 196616 | tf_op jit(solution)/shard_map/while/body/eval_jaxpr/ppermute | solution.py:12
  392.7 13.2 %collective-permute-start.1 = (bf16[2,128,128]{2,1,0:T(8,128)(2,1)S(1)}, bf16[2,128,128]{2,1,0:T(8,128)(2,1)S(1)}, u32[]{:S(2)}, u32[]{:S(2)}) collective-permute-start(bf16[2,128,128]{2,1,0:T(8,128)(2,1)S(1)} %get-tuple-element.332), channel_id=1, source_target_pairs={{0,8},{8,16},{16,24},{24,32},{32,40},{40,48},{48,56},{56,64},{64,7... | collective-permute-start | bytes 196616 | tf_op jit(solution)/shard_map/while/body/eval_jaxpr/ppermute | solution.py:12
  406.5 13.2 %collective-permute-start.1 = (bf16[2,128,128]{2,1,0:T(8,128)(2,1)S(1)}, bf16[2,128,128]{2,1,0:T(8,128)(2,1)S(1)}, u32[]{:S(2)}, u32[]{:S(2)}) collective-permute-start(bf16[2,128,128]{2,1,0:T(8,128)(2,1)S(1)} %get-tuple-element.332), channel_id=1, source_target_pairs={{0,8},{8,16},{16,24},{24,32},{32,40},{40,48},{48,56},{56,64},{64,7... | collective-permute-start | bytes 196616 | tf_op jit(solution)/shard_map/while/body/eval_jaxpr/ppermute | solution.py:12
  420.3 13.2 %collective-permute-start.1 = (bf16[2,128,128]{2,1,0:T(8,128)(2,1)S(1)}, bf16[2,128,128]{2,1,0:T(8,128)(2,1)S(1)}, u32[]{:S(2)}, u32[]{:S(2)}) collective-permute-start(bf16[2,128,128]{2,1,0:T(8,128)(2,1)S(1)} %get-tuple-element.332), channel_id=1, source_target_pairs={{0,8},{8,16},{16,24},{24,32},{32,40},{40,48},{48,56},{56,64},{64,7... | collective-permute-start | bytes 196616 | tf_op jit(solution)/shard_map/while/body/eval_jaxpr/ppermute | solution.py:12
  434.2 13.2 %collective-permute-start.1 = (bf16[2,128,128]{2,1,0:T(8,128)(2,1)S(1)}, bf16[2,128,128]{2,1,0:T(8,128)(2,1)S(1)}, u32[]{:S(2)}, u32[]{:S(2)}) collective-permute-start(bf16[2,128,128]{2,1,0:T(8,128)(2,1)S(1)} %get-tuple-element.332), channel_id=1, source_target_pairs={{0,8},{8,16},{16,24},{24,32},{32,40},{40,48},{48,56},{56,64},{64,7... | collective-permute-start | bytes 196616 | tf_op jit(solution)/shard_map/while/body/eval_jaxpr/ppermute | solution.py:12
  448.0 13.2 %collective-permute-start.1 = (bf16[2,128,128]{2,1,0:T(8,128)(2,1)S(1)}, bf16[2,128,128]{2,1,0:T(8,128)(2,1)S(1)}, u32[]{:S(2)}, u32[]{:S(2)}) collective-permute-start(bf16[2,128,128]{2,1,0:T(8,128)(2,1)S(1)} %get-tuple-element.332), channel_id=1, source_target_pairs={{0,8},{8,16},{16,24},{24,32},{32,40},{40,48},{48,56},{56,64},{64,7... | collective-permute-start | bytes 196616 | tf_op jit(solution)/shard_map/while/body/eval_jaxpr/ppermute | solution.py:12
  586.4 13.2 %collective-permute-start.1 = (bf16[2,128,128]{2,1,0:T(8,128)(2,1)S(1)}, bf16[2,128,128]{2,1,0:T(8,128)(2,1)S(1)}, u32[]{:S(2)}, u32[]{:S(2)}) collective-permute-start(bf16[2,128,128]{2,1,0:T(8,128)(2,1)S(1)} %get-tuple-element.332), channel_id=1, source_target_pairs={{0,8},{8,16},{16,24},{24,32},{32,40},{40,48},{48,56},{56,64},{64,7... | collective-permute-start | bytes 196616 | tf_op jit(solution)/shard_map/while/body/eval_jaxpr/ppermute | solution.py:12
  614.0 13.2 %collective-permute-start.1 = (bf16[2,128,128]{2,1,0:T(8,128)(2,1)S(1)}, bf16[2,128,128]{2,1,0:T(8,128)(2,1)S(1)}, u32[]{:S(2)}, u32[]{:S(2)}) collective-permute-start(bf16[2,128,128]{2,1,0:T(8,128)(2,1)S(1)} %get-tuple-element.332), channel_id=1, source_target_pairs={{0,8},{8,16},{16,24},{24,32},{32,40},{40,48},{48,56},{56,64},{64,7... | collective-permute-start | bytes 196616 | tf_op jit(solution)/shard_map/while/body/eval_jaxpr/ppermute | solution.py:12
  849.2 13.2 %collective-permute-start.1 = (bf16[2,128,128]{2,1,0:T(8,128)(2,1)S(1)}, bf16[2,128,128]{2,1,0:T(8,128)(2,1)S(1)}, u32[]{:S(2)}, u32[]{:S(2)}) collective-permute-start(bf16[2,128,128]{2,1,0:T(8,128)(2,1)S(1)} %get-tuple-element.332), channel_id=1, source_target_pairs={{0,8},{8,16},{16,24},{24,32},{32,40},{40,48},{48,56},{56,64},{64,7... | collective-permute-start | bytes 196616 | tf_op jit(solution)/shard_map/while/body/eval_jaxpr/ppermute | solution.py:12
  876.9 13.2 %collective-permute-start.1 = (bf16[2,128,128]{2,1,0:T(8,128)(2,1)S(1)}, bf16[2,128,128]{2,1,0:T(8,128)(2,1)S(1)}, u32[]{:S(2)}, u32[]{:S(2)}) collective-permute-start(bf16[2,128,128]{2,1,0:T(8,128)(2,1)S(1)} %get-tuple-element.332), channel_id=1, source_target_pairs={{0,8},{8,16},{16,24},{24,32},{32,40},{40,48},{48,56},{56,64},{64,7... | collective-permute-start | bytes 196616 | tf_op jit(solution)/shard_map/while/body/eval_jaxpr/ppermute | solution.py:12
  (102 other events, 2733.9 us)
Sparse Core Ops, SparseCore 0:
  9.4 63.3 all-gather.1
